TPU v7x, 32 devices: a whole 2x2x4 slice. The times are simulated.
32 devices in a mesh: grp: 2 (over x), blk: 16 (over z, y, core).
Axes of the slice: x: 2, y: 2, z: 4, core: 2. Of those that a mesh axis runs over, the one named last changes fastest.
Arguments:
- tokens: bfloat16 [16384, 1024], P(('grp', 'blk')), parts along dimension 0, may hold values from -6 to 6
- patch_of_row: int32 [16384], P(('grp', 'blk')), parts along dimension 0, may hold values from 0 to 2047, as said below
- latents: bfloat16 [256, 1024], P('blk'), may hold values from -110 to 110
- contrast_gain: bfloat16 [4, 1024], replicated, may hold values from 0.099609375 to 1.8984375
- norm_gain: bfloat16 [1024], replicated, may hold values from 0.099609375 to 1.8984375
- w_query: bfloat16 [1024, 1024], replicated, may hold values from -0.1875 to 0.1875
- w_key: bfloat16 [1024, 1024], replicated, may hold values from -0.1875 to 0.1875
- w_value: bfloat16 [1024, 1024], replicated, may hold values from -0.1875 to 0.1875
- w_out: bfloat16 [1024, 1024], replicated, may hold values from -0.1875 to 0.1875
Outputs:
- new_latents: bfloat16 [512, 1024], P(('grp', 'blk')), parts along dimension 0
There are 2 independent parts, one for each index of `grp`. A program takes and returns all parts, laid end to end along the dimension named above; an argument that names none is the same for every part. Nothing has to cross between parts.
Inputs may be any that keep to these rules, and one draw needn't show every extreme that they name: `patch_of_row`: for each contrast c, rows c * 2048 to (c + 1) * 2048 - 1 name every patch once, and row c * 2048 + s names a patch p with p // 128 == s % 16.
All inputs are finite; a program needn't handle non-finite values.
Results may differ from a plain program's by a relative error of at most 0.0065.
Values may be sent and summed in bfloat16 or wider, within the bound.
No kernel may reach another device: no remote copies, remote signals or barrier semaphores. Data moves between devices by JAX's collectives and lax.ppermute only.
A program may use at most 64 MiB of HBM per device.

v0:
```python
import jax
import jax.numpy as jnp
from jax import lax
from jax.sharding import PartitionSpec as P

HEADS = 16
CONTRASTS = 4


def shifted(block, axis, distance):
    devices = range(lax.axis_size(axis))
    route = [((i - distance) % len(devices), i) for i in devices]
    return lax.ppermute(block, axis, route)


def absorb(tile, maxima, totals, accum, key_heads, value_heads):
    tile_rows, model_width = tile.shape
    head_count, head_width = (key_heads.shape[1], key_heads.shape[2])
    tile_heads = tile.reshape(tile_rows, head_count, head_width)
    scores = jnp.einsum("lhd,khd->lhk", tile_heads, key_heads, preferred_element_type=jnp.float32)
    raised = jnp.maximum(maxima, jnp.max(scores, axis=-1))
    factor = jnp.exp(maxima - raised)
    weights = jnp.exp(scores - raised[..., None])
    totals = totals * factor + jnp.sum(weights, axis=-1)
    summed = jnp.einsum(
        "lhk,khd->lhd",
        weights.astype(jnp.bfloat16),
        value_heads,
        preferred_element_type=jnp.float32,
    )
    accum = accum.reshape(tile_rows, head_count, head_width) * factor[..., None] + summed
    return (raised, totals, accum.reshape(tile_rows, model_width))


def fresh_state(tile_rows, head_count, model_width):
    return (
        jnp.full((tile_rows, head_count), -1e30, jnp.float32),
        jnp.zeros((tile_rows, head_count), jnp.float32),
        jnp.zeros((tile_rows, model_width), jnp.float32),
    )


def pass_one(state):
    return (
        shifted(state[0].astype(jnp.bfloat16), "blk", 1).astype(jnp.float32),
        shifted(state[1].astype(jnp.bfloat16), "blk", 1).astype(jnp.float32),
        shifted(state[2].astype(jnp.bfloat16), "blk", 1).astype(jnp.float32),
    )


def local(tokens, patch_of_row, latents, contrast_gain, norm_gain, w_query, w_key, w_value, w_out):
    cycle_size = lax.axis_size("blk")
    my_index = lax.axis_index("blk")
    tok_rows, model_width = tokens.shape
    head_count = HEADS
    head_width = model_width // head_count
    per_peer = tok_rows // cycle_size
    patches_dev = tok_rows // CONTRASTS
    received = lax.all_to_all(
        tokens.reshape(per_peer, cycle_size, model_width),
        "blk",
        split_axis=1,
        concat_axis=1,
        tiled=True,
    )
    received_ids = lax.all_to_all(
        patch_of_row.reshape(per_peer, cycle_size), "blk", split_axis=1, concat_axis=1, tiled=True
    )
    source_dev = lax.broadcasted_iota(jnp.int32, (per_peer, cycle_size), 1)
    row_step = lax.broadcasted_iota(jnp.int32, (per_peer, cycle_size), 0)
    slot_index = source_dev * tok_rows + my_index + cycle_size * row_step
    contrast_id = slot_index // (patches_dev * cycle_size)
    target_row = (contrast_id * patches_dev + received_ids - my_index * patches_dev).reshape(
        tok_rows
    )
    inverse = (
        jnp.zeros((tok_rows,), jnp.int32).at[target_row].set(jnp.arange(tok_rows, dtype=jnp.int32))
    )
    arranged = received.reshape(tok_rows, model_width)[inverse].reshape(
        CONTRASTS, patches_dev, model_width
    )
    joined = jnp.sum(
        arranged.astype(jnp.float32) * contrast_gain.astype(jnp.float32)[:, None, :], axis=0
    )
    inverse_rms = lax.rsqrt(jnp.mean(joined * joined, axis=-1, keepdims=True) + 1e-05)
    normed = (joined * inverse_rms * norm_gain.astype(jnp.float32)).astype(jnp.bfloat16)
    key_rows = jnp.dot(normed, w_key, preferred_element_type=jnp.float32).astype(jnp.bfloat16)
    value_rows = jnp.dot(normed, w_value, preferred_element_type=jnp.float32).astype(jnp.bfloat16)
    key_heads = key_rows.reshape(patches_dev, head_count, head_width)
    value_heads = value_rows.reshape(patches_dev, head_count, head_width)
    queries = (
        jnp.dot(latents, w_query, preferred_element_type=jnp.float32) * head_width ** (-0.5)
    ).astype(jnp.bfloat16)
    lat_rows = latents.shape[0]

    def hop_step(index_hop, state_carry):
        tile, maxima, totals, accum = state_carry
        state = absorb(tile, maxima, totals, accum, key_heads, value_heads)
        tile = shifted(tile, "blk", 1)
        maxima, totals, accum = pass_one(state)
        return (tile, maxima, totals, accum)

    begin = (queries,) + fresh_state(lat_rows, head_count, model_width)
    tile, maxima, totals, accum = lax.fori_loop(0, cycle_size - 1, hop_step, begin)
    maxima, totals, accum = pass_one(absorb(tile, maxima, totals, accum, key_heads, value_heads))
    attended = (
        (accum.reshape(lat_rows, head_count, head_width) / totals[..., None])
        .reshape(lat_rows, model_width)
        .astype(jnp.bfloat16)
    )
    mixed = latents.astype(jnp.float32) + jnp.dot(
        attended, w_out, preferred_element_type=jnp.float32
    )
    return mixed.astype(jnp.bfloat16)


def solution(mesh):
    in_specs = (
        P(("grp", "blk"), None),
        P(("grp", "blk")),
        P("blk", None),
        P(),
        P(),
        P(),
        P(),
        P(),
        P(),
    )
    out_specs = P(("grp", "blk"), None)
    return jax.shard_map(local, mesh=mesh, in_specs=in_specs, out_specs=out_specs, check_vma=False)
```

profile of v0, /device:TPU:0, one launch (start us, length us, event | category | flops | bytes accessed | tf_op | source)
XLA Modules:
  0.0 180.4 jit_solution(3693052724654784124)
XLA Ops:
  1.6 7.4 %all-to-all-start.1 = ((s32[32,16,1]{0,2,1:T(1,128)}), s32[32,16,1]{0,2,1:T(1,128)S(1)}, u32[]{:S(2)}, u32[]{:S(2)}) async-start(s32[32,16,1]{0,2,1:T(1,128)} %copy.56), calls=%async_computation.1 | async-start | bytes 16384 | tf_op jit(solution)/shard_map/all_to_all | solution.py:66
  9.0 2.8 %copy.54 = bf16[32,16,1024]{2,0,1:T(8,128)(2,1)} copy(bf16[32,16,1024]{2,1,0:T(8,128)(2,1)} %bitcast.44) | data formatting | bytes 2097152 | tf_op jit(solution)/shard_map/reshape | solution.py:60
  11.9 3.5 %all-to-all-done.1 = s32[32,16,1]{0,2,1:T(1,128)S(1)} async-done(((s32[32,16,1]{0,2,1:T(1,128)}), s32[32,16,1]{0,2,1:T(1,128)S(1)}, u32[]{:S(2)}, u32[]{:S(2)}) %all-to-all-start.1) | async-done | bytes 2080 | tf_op jit(solution)/shard_map/all_to_all | solution.py:66
  15.3 4.3 %all-to-all-start = ((bf16[32,16,1024]{2,0,1:T(8,128)(2,1)}), bf16[32,16,1024]{2,0,1:T(8,128)(2,1)}, u32[]{:S(2)}, u32[]{:S(2)}) async-start(bf16[32,16,1024]{2,0,1:T(8,128)(2,1)} %copy.54), calls=%async_computation | async-start | bytes 2097152 | tf_op jit(solution)/shard_map/all_to_all | solution.py:59
  24.6 18.0 %all-to-all-done = bf16[32,16,1024]{2,0,1:T(8,128)(2,1)} async-done(((bf16[32,16,1024]{2,0,1:T(8,128)(2,1)}), bf16[32,16,1024]{2,0,1:T(8,128)(2,1)}, u32[]{:S(2)}, u32[]{:S(2)}) %all-to-all-start) | async-done | bytes 1048608 | tf_op jit(solution)/shard_map/all_to_all | solution.py:59
  44.4 2.8 %gather_fusion = bf16[512,1024]{1,0:T(8,128)(2,1)} fusion(bf16[512,1024]{1,0:T(8,128)(2,1)S(1)} %bitcast.40, s32[1024]{0:T(1024)S(1)} %pad_clamp_fusion), kind=kCustom, calls=%fused_computation | custom fusion | bytes 2099200 | tf_op jit(solution)/shard_map/gather | solution.py:79
  51.9 118.4 %while.17 = (s32[]{:T(128)}, bf16[16,1024]{1,0:T(8,128)(2,1)S(1)}, f32[16,16]{0,1:T(8,128)S(1)}, f32[16,16]{0,1:T(8,128)S(1)}, f32[16,1024]{1,0:T(8,128)S(1)}, /...) while((s32[]{:T(128)}, bf16[16,1024]{1,0:T(8,128)(2,1)S(1)}, ...), condition=%wide.region_6.7_spmd.clone, body=%wide.region_3.6_spmd.clone.sunk | while | flops 8636675 | bytes 1955081 | solution.py:104
  58.0 2.7 %collective-permute-done.1 = bf16[16,16]{0,1:T(8,128)(2,1)S(1)} collective-permute-done((bf16[16,16]{0,1:T(8,128)(2,1)S(1)}, bf16[16,16]{0,1:T(8,128)(2,1)S(1)}, u32[]{:S(2)}, u32[]{:S(2)}) %collective-permute-start.1) | collective-permute-done | bytes 544 | tf_op jit(solution)/shard_map/while/body/eval_jaxpr/ppermute | solution.py:13
  65.6 3.6 %collective-permute-done.1 = bf16[16,16]{0,1:T(8,128)(2,1)S(1)} collective-permute-done((bf16[16,16]{0,1:T(8,128)(2,1)S(1)}, bf16[16,16]{0,1:T(8,128)(2,1)S(1)}, u32[]{:S(2)}, u32[]{:S(2)}) %collective-permute-start.1) | collective-permute-done | bytes 544 | tf_op jit(solution)/shard_map/while/body/eval_jaxpr/ppermute | solution.py:13
  71.8 5.2 %collective-permute-done.1 = bf16[16,16]{0,1:T(8,128)(2,1)S(1)} collective-permute-done((bf16[16,16]{0,1:T(8,128)(2,1)S(1)}, bf16[16,16]{0,1:T(8,128)(2,1)S(1)}, u32[]{:S(2)}, u32[]{:S(2)}) %collective-permute-start.1) | collective-permute-done | bytes 544 | tf_op jit(solution)/shard_map/while/body/eval_jaxpr/ppermute | solution.py:13
  78.5 6.2 %collective-permute-done.1 = bf16[16,16]{0,1:T(8,128)(2,1)S(1)} collective-permute-done((bf16[16,16]{0,1:T(8,128)(2,1)S(1)}, bf16[16,16]{0,1:T(8,128)(2,1)S(1)}, u32[]{:S(2)}, u32[]{:S(2)}) %collective-permute-start.1) | collective-permute-done | bytes 544 | tf_op jit(solution)/shard_map/while/body/eval_jaxpr/ppermute | solution.py:13
  86.3 6.2 %collective-permute-done.1 = bf16[16,16]{0,1:T(8,128)(2,1)S(1)} collective-permute-done((bf16[16,16]{0,1:T(8,128)(2,1)S(1)}, bf16[16,16]{0,1:T(8,128)(2,1)S(1)}, u32[]{:S(2)}, u32[]{:S(2)}) %collective-permute-start.1) | collective-permute-done | bytes 544 | tf_op jit(solution)/shard_map/while/body/eval_jaxpr/ppermute | solution.py:13
  94.1 6.2 %collective-permute-done.1 = bf16[16,16]{0,1:T(8,128)(2,1)S(1)} collective-permute-done((bf16[16,16]{0,1:T(8,128)(2,1)S(1)}, bf16[16,16]{0,1:T(8,128)(2,1)S(1)}, u32[]{:S(2)}, u32[]{:S(2)}) %collective-permute-start.1) | collective-permute-done | bytes 544 | tf_op jit(solution)/shard_map/while/body/eval_jaxpr/ppermute | solution.py:13
  101.8 6.2 %collective-permute-done.1 = bf16[16,16]{0,1:T(8,128)(2,1)S(1)} collective-permute-done((bf16[16,16]{0,1:T(8,128)(2,1)S(1)}, bf16[16,16]{0,1:T(8,128)(2,1)S(1)}, u32[]{:S(2)}, u32[]{:S(2)}) %collective-permute-start.1) | collective-permute-done | bytes 544 | tf_op jit(solution)/shard_map/while/body/eval_jaxpr/ppermute | solution.py:13
  109.6 6.2 %collective-permute-done.1 = bf16[16,16]{0,1:T(8,128)(2,1)S(1)} collective-permute-done((bf16[16,16]{0,1:T(8,128)(2,1)S(1)}, bf16[16,16]{0,1:T(8,128)(2,1)S(1)}, u32[]{:S(2)}, u32[]{:S(2)}) %collective-permute-start.1) | collective-permute-done | bytes 544 | tf_op jit(solution)/shard_map/while/body/eval_jaxpr/ppermute | solution.py:13
  117.3 6.2 %collective-permute-done.1 = bf16[16,16]{0,1:T(8,128)(2,1)S(1)} collective-permute-done((bf16[16,16]{0,1:T(8,128)(2,1)S(1)}, bf16[16,16]{0,1:T(8,128)(2,1)S(1)}, u32[]{:S(2)}, u32[]{:S(2)}) %collective-permute-start.1) | collective-permute-done | bytes 544 | tf_op jit(solution)/shard_map/while/body/eval_jaxpr/ppermute | solution.py:13
  125.1 6.2 %collective-permute-done.1 = bf16[16,16]{0,1:T(8,128)(2,1)S(1)} collective-permute-done((bf16[16,16]{0,1:T(8,128)(2,1)S(1)}, bf16[16,16]{0,1:T(8,128)(2,1)S(1)}, u32[]{:S(2)}, u32[]{:S(2)}) %collective-permute-start.1) | collective-permute-done | bytes 544 | tf_op jit(solution)/shard_map/while/body/eval_jaxpr/ppermute | solution.py:13
  132.9 6.2 %collective-permute-done.1 = bf16[16,16]{0,1:T(8,128)(2,1)S(1)} collective-permute-done((bf16[16,16]{0,1:T(8,128)(2,1)S(1)}, bf16[16,16]{0,1:T(8,128)(2,1)S(1)}, u32[]{:S(2)}, u32[]{:S(2)}) %collective-permute-start.1) | collective-permute-done | bytes 544 | tf_op jit(solution)/shard_map/while/body/eval_jaxpr/ppermute | solution.py:13
  140.6 6.2 %collective-permute-done.1 = bf16[16,16]{0,1:T(8,128)(2,1)S(1)} collective-permute-done((bf16[16,16]{0,1:T(8,128)(2,1)S(1)}, bf16[16,16]{0,1:T(8,128)(2,1)S(1)}, u32[]{:S(2)}, u32[]{:S(2)}) %collective-permute-start.1) | collective-permute-done | bytes 544 | tf_op jit(solution)/shard_map/while/body/eval_jaxpr/ppermute | solution.py:13
  148.4 6.2 %collective-permute-done.1 = bf16[16,16]{0,1:T(8,128)(2,1)S(1)} collective-permute-done((bf16[16,16]{0,1:T(8,128)(2,1)S(1)}, bf16[16,16]{0,1:T(8,128)(2,1)S(1)}, u32[]{:S(2)}, u32[]{:S(2)}) %collective-permute-start.1) | collective-permute-done | bytes 544 | tf_op jit(solution)/shard_map/while/body/eval_jaxpr/ppermute | solution.py:13
  156.2 6.2 %collective-permute-done.1 = bf16[16,16]{0,1:T(8,128)(2,1)S(1)} collective-permute-done((bf16[16,16]{0,1:T(8,128)(2,1)S(1)}, bf16[16,16]{0,1:T(8,128)(2,1)S(1)}, u32[]{:S(2)}, u32[]{:S(2)}) %collective-permute-start.1) | collective-permute-done | bytes 544 | tf_op jit(solution)/shard_map/while/body/eval_jaxpr/ppermute | solution.py:13
  163.9 6.2 %collective-permute-done.1 = bf16[16,16]{0,1:T(8,128)(2,1)S(1)} collective-permute-done((bf16[16,16]{0,1:T(8,128)(2,1)S(1)}, bf16[16,16]{0,1:T(8,128)(2,1)S(1)}, u32[]{:S(2)}, u32[]{:S(2)}) %collective-permute-start.1) | collective-permute-done | bytes 544 | tf_op jit(solution)/shard_map/while/body/eval_jaxpr/ppermute | solution.py:13
  171.5 6.0 %collective-permute-done.5 = bf16[16,16]{0,1:T(8,128)(2,1)S(1)} collective-permute-done((bf16[16,16]{0,1:T(8,128)(2,1)S(1)}, bf16[16,16]{0,1:T(8,128)(2,1)S(1)}, u32[]{:S(2)}, u32[]{:S(2)}) %collective-permute-start.5) | collective-permute-done | bytes 544 | tf_op jit(solution)/shard_map/ppermute | solution.py:13
  177.8 2.6 %fusion.13 = bf16[16,1024]{1,0:T(8,128)(2,1)} fusion(bf16[1024,1024]{1,0:T(8,128)(2,1)} %param.19, bf16[16,1024]{1,0:T(8,128)(2,1)S(1)} %copy-done.1, f32[16,1024]{1,0:T(8,128)S(1)} %div.36, bf16[16,1024]{1,0:T(8,128)(2,1)S(1)} %collective-permute-done.4), kind=kOutput, calls=%fused_computation.29 | convolution fusion | flops 33652736 | bytes 2260992 | tf_op jit(solution)/shard_map/dot_general | solution.py:111
  (369 shorter events, 44.7 us)
Async XLA Ops:
  1.6 13.7 %all-to-all-start.1 = ((s32[32,16,1]{0,2,1:T(1,128)}), s32[32,16,1]{0,2,1:T(1,128)S(1)}, u32[]{:S(2)}, u32[]{:S(2)}) async-start(s32[32,16,1]{0,2,1:T(1,128)} %copy.56), calls=%async_computation.1 | async-start | bytes 16384 | tf_op jit(solution)/shard_map/all_to_all | solution.py:66
  15.3 27.3 %all-to-all-start = ((bf16[32,16,1024]{2,0,1:T(8,128)(2,1)}), bf16[32,16,1024]{2,0,1:T(8,128)(2,1)}, u32[]{:S(2)}, u32[]{:S(2)}) async-start(bf16[32,16,1024]{2,0,1:T(8,128)(2,1)} %copy.54), calls=%async_computation | async-start | bytes 2097152 | tf_op jit(solution)/shard_map/all_to_all | solution.py:59
  53.1 8.5 %collective-permute-start.3 = (bf16[16,1024]{1,0:T(8,128)(2,1)S(1)}, bf16[16,1024]{1,0:T(8,128)(2,1)S(1)}, u32[]{:S(2)}, u32[]{:S(2)}) collective-permute-start(bf16[16,1024]{1,0:T(8,128)(2,1)S(1)} %convert_element_type.136), channel_id=1, source_target_pairs={{15,0},{0,1},{1,2},{2,3},{3,4},{4,5},{5,6},{6,7},{7,8},{8,9},{9,10... | collective-permute-start | bytes 98312 | tf_op jit(solution)/shard_map/while/body/eval_jaxpr/ppermute | solution.py:13
  53.7 7.8 %collective-permute-start = (bf16[16,1024]{1,0:T(8,128)(2,1)S(1)}, bf16[16,1024]{1,0:T(8,128)(2,1)S(1)}, u32[]{:S(2)}, u32[]{:S(2)}) collective-permute-start(bf16[16,1024]{1,0:T(8,128)(2,1)S(1)} %copy.90), channel_id=1, source_target_pairs={{15,0},{0,1},{1,2},{2,3},{3,4},{4,5},{5,6},{6,7},{7,8},{8,9},{9,10... | collective-permute-start | bytes 98312 | tf_op jit(solution)/shard_map/while/body/eval_jaxpr/ppermute | solution.py:13
  62.7 6.5 %collective-permute-start.3 = (bf16[16,1024]{1,0:T(8,128)(2,1)S(1)}, bf16[16,1024]{1,0:T(8,128)(2,1)S(1)}, u32[]{:S(2)}, u32[]{:S(2)}) collective-permute-start(bf16[16,1024]{1,0:T(8,128)(2,1)S(1)} %convert_element_type.136), channel_id=1, source_target_pairs={{15,0},{0,1},{1,2},{2,3},{3,4},{4,5},{5,6},{6,7},{7,8},{8,9},{9,10... | collective-permute-start | bytes 98312 | tf_op jit(solution)/shard_map/while/body/eval_jaxpr/ppermute | solution.py:13
  70.5 6.5 %collective-permute-start.3 = (bf16[16,1024]{1,0:T(8,128)(2,1)S(1)}, bf16[16,1024]{1,0:T(8,128)(2,1)S(1)}, u32[]{:S(2)}, u32[]{:S(2)}) collective-permute-start(bf16[16,1024]{1,0:T(8,128)(2,1)S(1)} %convert_element_type.136), channel_id=1, source_target_pairs={{15,0},{0,1},{1,2},{2,3},{3,4},{4,5},{5,6},{6,7},{7,8},{8,9},{9,10... | collective-permute-start | bytes 98312 | tf_op jit(solution)/shard_map/while/body/eval_jaxpr/ppermute | solution.py:13
  70.6 6.5 %collective-permute-start = (bf16[16,1024]{1,0:T(8,128)(2,1)S(1)}, bf16[16,1024]{1,0:T(8,128)(2,1)S(1)}, u32[]{:S(2)}, u32[]{:S(2)}) collective-permute-start(bf16[16,1024]{1,0:T(8,128)(2,1)S(1)} %copy.90), channel_id=1, source_target_pairs={{15,0},{0,1},{1,2},{2,3},{3,4},{4,5},{5,6},{6,7},{7,8},{8,9},{9,10... | collective-permute-start | bytes 98312 | tf_op jit(solution)/shard_map/while/body/eval_jaxpr/ppermute | solution.py:13
  78.3 6.5 %collective-permute-start.3 = (bf16[16,1024]{1,0:T(8,128)(2,1)S(1)}, bf16[16,1024]{1,0:T(8,128)(2,1)S(1)}, u32[]{:S(2)}, u32[]{:S(2)}) collective-permute-start(bf16[16,1024]{1,0:T(8,128)(2,1)S(1)} %convert_element_type.136), channel_id=1, source_target_pairs={{15,0},{0,1},{1,2},{2,3},{3,4},{4,5},{5,6},{6,7},{7,8},{8,9},{9,10... | collective-permute-start | bytes 98312 | tf_op jit(solution)/shard_map/while/body/eval_jaxpr/ppermute | solution.py:13
  86.0 6.5 %collective-permute-start.3 = (bf16[16,1024]{1,0:T(8,128)(2,1)S(1)}, bf16[16,1024]{1,0:T(8,128)(2,1)S(1)}, u32[]{:S(2)}, u32[]{:S(2)}) collective-permute-start(bf16[16,1024]{1,0:T(8,128)(2,1)S(1)} %convert_element_type.136), channel_id=1, source_target_pairs={{15,0},{0,1},{1,2},{2,3},{3,4},{4,5},{5,6},{6,7},{7,8},{8,9},{9,10... | collective-permute-start | bytes 98312 | tf_op jit(solution)/shard_map/while/body/eval_jaxpr/ppermute | solution.py:13
  86.1 6.5 %collective-permute-start = (bf16[16,1024]{1,0:T(8,128)(2,1)S(1)}, bf16[16,1024]{1,0:T(8,128)(2,1)S(1)}, u32[]{:S(2)}, u32[]{:S(2)}) collective-permute-start(bf16[16,1024]{1,0:T(8,128)(2,1)S(1)} %copy.90), channel_id=1, source_target_pairs={{15,0},{0,1},{1,2},{2,3},{3,4},{4,5},{5,6},{6,7},{7,8},{8,9},{9,10... | collective-permute-start | bytes 98312 | tf_op jit(solution)/shard_map/while/body/eval_jaxpr/ppermute | solution.py:13
  93.8 6.5 %collective-permute-start.3 = (bf16[16,1024]{1,0:T(8,128)(2,1)S(1)}, bf16[16,1024]{1,0:T(8,128)(2,1)S(1)}, u32[]{:S(2)}, u32[]{:S(2)}) collective-permute-start(bf16[16,1024]{1,0:T(8,128)(2,1)S(1)} %convert_element_type.136), channel_id=1, source_target_pairs={{15,0},{0,1},{1,2},{2,3},{3,4},{4,5},{5,6},{6,7},{7,8},{8,9},{9,10... | collective-permute-start | bytes 98312 | tf_op jit(solution)/shard_map/while/body/eval_jaxpr/ppermute | solution.py:13
  93.9 6.5 %collective-permute-start = (bf16[16,1024]{1,0:T(8,128)(2,1)S(1)}, bf16[16,1024]{1,0:T(8,128)(2,1)S(1)}, u32[]{:S(2)}, u32[]{:S(2)}) collective-permute-start(bf16[16,1024]{1,0:T(8,128)(2,1)S(1)} %copy.90), channel_id=1, source_target_pairs={{15,0},{0,1},{1,2},{2,3},{3,4},{4,5},{5,6},{6,7},{7,8},{8,9},{9,10... | collective-permute-start | bytes 98312 | tf_op jit(solution)/shard_map/while/body/eval_jaxpr/ppermute | solution.py:13
  101.6 6.5 %collective-permute-start.3 = (bf16[16,1024]{1,0:T(8,128)(2,1)S(1)}, bf16[16,1024]{1,0:T(8,128)(2,1)S(1)}, u32[]{:S(2)}, u32[]{:S(2)}) collective-permute-start(bf16[16,1024]{1,0:T(8,128)(2,1)S(1)} %convert_element_type.136), channel_id=1, source_target_pairs={{15,0},{0,1},{1,2},{2,3},{3,4},{4,5},{5,6},{6,7},{7,8},{8,9},{9,10... | collective-permute-start | bytes 98312 | tf_op jit(solution)/shard_map/while/body/eval_jaxpr/ppermute | solution.py:13
  101.6 6.5 %collective-permute-start = (bf16[16,1024]{1,0:T(8,128)(2,1)S(1)}, bf16[16,1024]{1,0:T(8,128)(2,1)S(1)}, u32[]{:S(2)}, u32[]{:S(2)}) collective-permute-start(bf16[16,1024]{1,0:T(8,128)(2,1)S(1)} %copy.90), channel_id=1, source_target_pairs={{15,0},{0,1},{1,2},{2,3},{3,4},{4,5},{5,6},{6,7},{7,8},{8,9},{9,10... | collective-permute-start | bytes 98312 | tf_op jit(solution)/shard_map/while/body/eval_jaxpr/ppermute | solution.py:13
  109.3 6.5 %collective-permute-start.3 = (bf16[16,1024]{1,0:T(8,128)(2,1)S(1)}, bf16[16,1024]{1,0:T(8,128)(2,1)S(1)}, u32[]{:S(2)}, u32[]{:S(2)}) collective-permute-start(bf16[16,1024]{1,0:T(8,128)(2,1)S(1)} %convert_element_type.136), channel_id=1, source_target_pairs={{15,0},{0,1},{1,2},{2,3},{3,4},{4,5},{5,6},{6,7},{7,8},{8,9},{9,10... | collective-permute-start | bytes 98312 | tf_op jit(solution)/shard_map/while/body/eval_jaxpr/ppermute | solution.py:13
  117.1 6.5 %collective-permute-start.3 = (bf16[16,1024]{1,0:T(8,128)(2,1)S(1)}, bf16[16,1024]{1,0:T(8,128)(2,1)S(1)}, u32[]{:S(2)}, u32[]{:S(2)}) collective-permute-start(bf16[16,1024]{1,0:T(8,128)(2,1)S(1)} %convert_element_type.136), channel_id=1, source_target_pairs={{15,0},{0,1},{1,2},{2,3},{3,4},{4,5},{5,6},{6,7},{7,8},{8,9},{9,10... | collective-permute-start | bytes 98312 | tf_op jit(solution)/shard_map/while/body/eval_jaxpr/ppermute | solution.py:13
  117.1 6.5 %collective-permute-start = (bf16[16,1024]{1,0:T(8,128)(2,1)S(1)}, bf16[16,1024]{1,0:T(8,128)(2,1)S(1)}, u32[]{:S(2)}, u32[]{:S(2)}) collective-permute-start(bf16[16,1024]{1,0:T(8,128)(2,1)S(1)} %copy.90), channel_id=1, source_target_pairs={{15,0},{0,1},{1,2},{2,3},{3,4},{4,5},{5,6},{6,7},{7,8},{8,9},{9,10... | collective-permute-start | bytes 98312 | tf_op jit(solution)/shard_map/while/body/eval_jaxpr/ppermute | solution.py:13
  124.8 6.5 %collective-permute-start.3 = (bf16[16,1024]{1,0:T(8,128)(2,1)S(1)}, bf16[16,1024]{1,0:T(8,128)(2,1)S(1)}, u32[]{:S(2)}, u32[]{:S(2)}) collective-permute-start(bf16[16,1024]{1,0:T(8,128)(2,1)S(1)} %convert_element_type.136), channel_id=1, source_target_pairs={{15,0},{0,1},{1,2},{2,3},{3,4},{4,5},{5,6},{6,7},{7,8},{8,9},{9,10... | collective-permute-start | bytes 98312 | tf_op jit(solution)/shard_map/while/body/eval_jaxpr/ppermute | solution.py:13
  124.9 6.5 %collective-permute-start = (bf16[16,1024]{1,0:T(8,128)(2,1)S(1)}, bf16[16,1024]{1,0:T(8,128)(2,1)S(1)}, u32[]{:S(2)}, u32[]{:S(2)}) collective-permute-start(bf16[16,1024]{1,0:T(8,128)(2,1)S(1)} %copy.90), channel_id=1, source_target_pairs={{15,0},{0,1},{1,2},{2,3},{3,4},{4,5},{5,6},{6,7},{7,8},{8,9},{9,10... | collective-permute-start | bytes 98312 | tf_op jit(solution)/shard_map/while/body/eval_jaxpr/ppermute | solution.py:13
  132.6 6.5 %collective-permute-start.3 = (bf16[16,1024]{1,0:T(8,128)(2,1)S(1)}, bf16[16,1024]{1,0:T(8,128)(2,1)S(1)}, u32[]{:S(2)}, u32[]{:S(2)}) collective-permute-start(bf16[16,1024]{1,0:T(8,128)(2,1)S(1)} %convert_element_type.136), channel_id=1, source_target_pairs={{15,0},{0,1},{1,2},{2,3},{3,4},{4,5},{5,6},{6,7},{7,8},{8,9},{9,10... | collective-permute-start | bytes 98312 | tf_op jit(solution)/shard_map/while/body/eval_jaxpr/ppermute | solution.py:13
  140.4 6.5 %collective-permute-start.3 = (bf16[16,1024]{1,0:T(8,128)(2,1)S(1)}, bf16[16,1024]{1,0:T(8,128)(2,1)S(1)}, u32[]{:S(2)}, u32[]{:S(2)}) collective-permute-start(bf16[16,1024]{1,0:T(8,128)(2,1)S(1)} %convert_element_type.136), channel_id=1, source_target_pairs={{15,0},{0,1},{1,2},{2,3},{3,4},{4,5},{5,6},{6,7},{7,8},{8,9},{9,10... | collective-permute-start | bytes 98312 | tf_op jit(solution)/shard_map/while/body/eval_jaxpr/ppermute | solution.py:13
  148.1 6.5 %collective-permute-start.3 = (bf16[16,1024]{1,0:T(8,128)(2,1)S(1)}, bf16[16,1024]{1,0:T(8,128)(2,1)S(1)}, u32[]{:S(2)}, u32[]{:S(2)}) collective-permute-start(bf16[16,1024]{1,0:T(8,128)(2,1)S(1)} %convert_element_type.136), channel_id=1, source_target_pairs={{15,0},{0,1},{1,2},{2,3},{3,4},{4,5},{5,6},{6,7},{7,8},{8,9},{9,10... | collective-permute-start | bytes 98312 | tf_op jit(solution)/shard_map/while/body/eval_jaxpr/ppermute | solution.py:13
  155.9 6.5 %collective-permute-start.3 = (bf16[16,1024]{1,0:T(8,128)(2,1)S(1)}, bf16[16,1024]{1,0:T(8,128)(2,1)S(1)}, u32[]{:S(2)}, u32[]{:S(2)}) collective-permute-start(bf16[16,1024]{1,0:T(8,128)(2,1)S(1)} %convert_element_type.136), channel_id=1, source_target_pairs={{15,0},{0,1},{1,2},{2,3},{3,4},{4,5},{5,6},{6,7},{7,8},{8,9},{9,10... | collective-permute-start | bytes 98312 | tf_op jit(solution)/shard_map/while/body/eval_jaxpr/ppermute | solution.py:13
  163.7 6.5 %collective-permute-start.3 = (bf16[16,1024]{1,0:T(8,128)(2,1)S(1)}, bf16[16,1024]{1,0:T(8,128)(2,1)S(1)}, u32[]{:S(2)}, u32[]{:S(2)}) collective-permute-start(bf16[16,1024]{1,0:T(8,128)(2,1)S(1)} %convert_element_type.136), channel_id=1, source_target_pairs={{15,0},{0,1},{1,2},{2,3},{3,4},{4,5},{5,6},{6,7},{7,8},{8,9},{9,10... | collective-permute-start | bytes 98312 | tf_op jit(solution)/shard_map/while/body/eval_jaxpr/ppermute | solution.py:13
  (46 other events, 363.9 us)
where the time goes:
time: 181 us; the launch traced here: 180 us
  waiting for transfers between devices  115 us (64%)
  starting transfers between devices  23.6 us (13%)
  local copies, waits for them, and re-layouts  17.7 us (10%)
  matrix products  16.3 us (9%)
  other arithmetic  5.59 us (3%)
    ppermute x62, waiting for transfers between devices, shifted(): return lax.ppermute(block, axis, route)  93.7 us
    all_to_all x1, waiting for transfers between devices, local(): lax.all_to_all(tokens.reshape(per_peer, cycle_size, model_width), 'blk',...  18 us
    ppermute x62, starting transfers between devices, shifted(): return lax.ppermute(block, axis, route)  11.9 us
    all_to_all x1, starting transfers between devices, local(): lax.all_to_all(patch_of_row.reshape(per_peer, cycle_size), 'blk', split_a...  7.39 us
    dot_general x16, matrix products, absorb(): jnp.einsum('lhk,khd->lhd', weights.astype(jnp.bfloat16), value_heads, pre...  5.02 us
    all_to_all x1, starting transfers between devices, local(): lax.all_to_all(tokens.reshape(per_peer, cycle_size, model_width), 'blk',...  4.33 us
    dot_general x16, matrix products, absorb(): jnp.einsum('lhd,khd->lhk', tile_heads, key_heads, preferred_element_type=...  4.1 us
  transfers between devices with their start and end apart: 64, of which 19 were waited for; matrix products, arithmetic and copies ran while one was open for 4% of the time, Pallas kernels for 0%

commit v1 on v0

--- a/solution.py
+++ b/solution.py
@@ -1,3 +1,4 @@
+import functools
 import jax
 import jax.numpy as jnp
 from jax import lax
@@ -5,6 +6,16 @@
 
 HEADS = 16
 CONTRASTS = 4
+
+
+def read_outputs(local_values, shard_axis):
+    vec_out = lax.psum(1, shard_axis)
+    local_next = jnp.split(local_values, vec_out, axis=1)
+    base_arr = lax.all_to_all(jnp.stack(local_next), shard_axis, 0, 0)
+    return jnp.concatenate(base_arr, axis=1)
+
+
+rest_the_sizes = functools.partial(read_outputs, shard_axis="blk")
 
 
 def shifted(block, axis, distance):
@@ -56,13 +67,7 @@
     head_width = model_width // head_count
     per_peer = tok_rows // cycle_size
     patches_dev = tok_rows // CONTRASTS
-    received = lax.all_to_all(
-        tokens.reshape(per_peer, cycle_size, model_width),
-        "blk",
-        split_axis=1,
-        concat_axis=1,
-        tiled=True,
-    )
+    received = rest_the_sizes(tokens.reshape(per_peer, cycle_size, model_width))
     received_ids = lax.all_to_all(
         patch_of_row.reshape(per_peer, cycle_size), "blk", split_axis=1, concat_axis=1, tiled=True
     )

time: 181 us -> 193 us (1.066)
  local copies, waits for them, and re-layouts: 17.7 us -> 31.2 us
  waiting for transfers between devices: 115 us -> 111 us
    unnamed x12 -> x25, local copies, waits for them, and re-layouts: 0.1 us -> 9.77 us
    split x0 -> x1, local copies, waits for them, and re-layouts: none -> 6.01 us  [read_outputs(): local_next = jnp.split(local_values, vec_out, axis=1)]
    all_to_all x1, waiting for transfers between devices: 3.46 us -> 0.01 us  [local(): lax.all_to_all(patch_of_row.reshape(per_peer, cycle_size), 'blk', split_a...]
  transfers between devices with their start and end apart: 64 -> 64, of which waited for: 19 -> 18; matrix products, arithmetic and copies ran while one was open for 4% -> 12% of each run, Pallas kernels for 0% -> 0%
where the time goes in v1:
time: 193 us; the launch traced here: 192 us
  waiting for transfers between devices  111 us (58%)
  local copies, waits for them, and re-layouts  31.2 us (16%)
  starting transfers between devices  25.3 us (13%)
  matrix products  16.3 us (8%)
  other arithmetic  6.18 us (3%)
    ppermute x62, waiting for transfers between devices, shifted(): return lax.ppermute(block, axis, route)  93.6 us
    all_to_all x1, waiting for transfers between devices, read_outputs(): base_arr = lax.all_to_all(jnp.stack(local_next), shard_axis, 0, 0)  17.5 us
    ppermute x62, starting transfers between devices, shifted(): return lax.ppermute(block, axis, route)  11.9 us
    unnamed x25, local copies, waits for them, and re-layouts  9.77 us
    all_to_all x1, starting transfers between devices, local(): lax.all_to_all(patch_of_row.reshape(per_peer, cycle_size), 'blk', split_a...  7.39 us
    all_to_all x1, starting transfers between devices, read_outputs(): base_arr = lax.all_to_all(jnp.stack(local_next), shard_axis, 0, 0)  6.04 us
    split x1, local copies, waits for them, and re-layouts, read_outputs(): local_next = jnp.split(local_values, vec_out, axis=1)  6.01 us
    dot_general x16, matrix products, absorb(): jnp.einsum('lhk,khd->lhd', weights.astype(jnp.bfloat16), value_heads, pre...  5.02 us
  transfers between devices with their start and end apart: 64, of which 18 were waited for; matrix products, arithmetic and copies ran while one was open for 12% of the time, Pallas kernels for 0%

profile of v1, /device:TPU:0, one launch (start us, length us, event | category | flops | bytes accessed | tf_op | source)
XLA Modules:
  0.0 192.2 jit_solution(8797374758111460095)
XLA Ops:
  1.6 7.4 %all-to-all-start.1 = ((s32[32,16,1]{0,2,1:T(1,128)}), s32[32,16,1]{0,2,1:T(1,128)S(1)}, u32[]{:S(2)}, u32[]{:S(2)}) async-start(s32[32,16,1]{0,2,1:T(1,128)} %copy.69), calls=%async_computation.1 | async-start | bytes 16384 | tf_op jit(solution)/shard_map/all_to_all | solution.py:71
  9.0 6.0 %fusion.23 = (bf16[32,1,1024]{2,1,0:T(2,128)(2,1)S(1)}, bf16[32,1,1024]{2,1,0:T(2,128)(2,1)S(1)}, bf16[32,1,1024]{2,1,0:T(2,128)(2,1)S(1)}, bf16[32,1,1024]{2,1,...) fusion(bf16[32,16,1024]{2,1,0:T(8,128)(2,1)} %bitcast.77), kind=kLoop, calls=%fused_computation.72 | loop fusion | bytes 2097152 | tf_op jit(solution)/shard_map/split | solution.py:13
  25.4 6.0 %all-to-all-start = ((bf16[16,32,1,1024]{3,1,2,0:T(8,128)(2,1)}), bf16[16,32,1,1024]{3,1,2,0:T(8,128)(2,1)}, u32[]{:S(2)}, u32[]{:S(2)}) async-start(bf16[16,32,1,1024]{3,1,2,0:T(8,128)(2,1)} %bitcast_dynamic-update-slice_fusion), calls=%async_computation | async-start | bytes 2097152 | tf_op jit(solution)/shard_map/all_to_all | solution.py:14
  34.5 2.4 %scatter_custom_fusion = s32[512]{0:T(512)S(1)} fusion(s32[512]{0:T(512)S(1)} %bitcast.78, s32[512]{0:T(512)S(1)} %iota.19, s32[]{:T(128)} %constant.23.clone.1), kind=kCustom, calls=%fused_computation.65 | custom fusion | bytes 2052 | tf_op jit(solution)/shard_map/scatter | solution.py:82
  37.0 17.5 %all-to-all-done = bf16[16,32,1,1024]{3,1,2,0:T(8,128)(2,1)} async-done(((bf16[16,32,1,1024]{3,1,2,0:T(8,128)(2,1)}), bf16[16,32,1,1024]{3,1,2,0:T(8,128)(2,1)}, u32[]{:S(2)}, u32[]{:S(2)}) %all-to-all-start) | async-done | bytes 1048608 | tf_op jit(solution)/shard_map/all_to_all | solution.py:14
  56.3 2.8 %gather_fusion = bf16[512,1024]{1,0:T(8,128)(2,1)} fusion(bf16[512,1024]{1,0:T(8,128)(2,1)S(1)} %bitcast.73, s32[1024]{0:T(1024)S(1)} %pad_clamp_fusion), kind=kCustom, calls=%fused_computation | custom fusion | bytes 2099200 | tf_op jit(solution)/shard_map/gather | solution.py:84
  63.6 118.4 %while.17 = (s32[]{:T(128)}, bf16[16,1024]{1,0:T(8,128)(2,1)S(1)}, f32[16,16]{0,1:T(8,128)S(1)}, f32[16,16]{0,1:T(8,128)S(1)}, f32[16,1024]{1,0:T(8,128)S(1)}, /...) while((s32[]{:T(128)}, bf16[16,1024]{1,0:T(8,128)(2,1)S(1)}, ...), condition=%wide.region_6.7_spmd.clone, body=%wide.region_3.6_spmd.clone.sunk | while | flops 8636675 | bytes 1955081 | solution.py:109
  69.8 2.7 %collective-permute-done.2 = bf16[16,16]{0,1:T(8,128)(2,1)S(1)} collective-permute-done((bf16[16,16]{0,1:T(8,128)(2,1)S(1)}, bf16[16,16]{0,1:T(8,128)(2,1)S(1)}, u32[]{:S(2)}, u32[]{:S(2)}) %collective-permute-start.2) | collective-permute-done | bytes 544 | tf_op jit(solution)/shard_map/while/body/eval_jaxpr/ppermute | solution.py:24
  77.4 3.6 %collective-permute-done.2 = bf16[16,16]{0,1:T(8,128)(2,1)S(1)} collective-permute-done((bf16[16,16]{0,1:T(8,128)(2,1)S(1)}, bf16[16,16]{0,1:T(8,128)(2,1)S(1)}, u32[]{:S(2)}, u32[]{:S(2)}) %collective-permute-start.2) | collective-permute-done | bytes 544 | tf_op jit(solution)/shard_map/while/body/eval_jaxpr/ppermute | solution.py:24
  83.6 5.2 %collective-permute-done.2 = bf16[16,16]{0,1:T(8,128)(2,1)S(1)} collective-permute-done((bf16[16,16]{0,1:T(8,128)(2,1)S(1)}, bf16[16,16]{0,1:T(8,128)(2,1)S(1)}, u32[]{:S(2)}, u32[]{:S(2)}) %collective-permute-start.2) | collective-permute-done | bytes 544 | tf_op jit(solution)/shard_map/while/body/eval_jaxpr/ppermute | solution.py:24
  90.3 6.2 %collective-permute-done.2 = bf16[16,16]{0,1:T(8,128)(2,1)S(1)} collective-permute-done((bf16[16,16]{0,1:T(8,128)(2,1)S(1)}, bf16[16,16]{0,1:T(8,128)(2,1)S(1)}, u32[]{:S(2)}, u32[]{:S(2)}) %collective-permute-start.2) | collective-permute-done | bytes 544 | tf_op jit(solution)/shard_map/while/body/eval_jaxpr/ppermute | solution.py:24
  98.1 6.2 %collective-permute-done.2 = bf16[16,16]{0,1:T(8,128)(2,1)S(1)} collective-permute-done((bf16[16,16]{0,1:T(8,128)(2,1)S(1)}, bf16[16,16]{0,1:T(8,128)(2,1)S(1)}, u32[]{:S(2)}, u32[]{:S(2)}) %collective-permute-start.2) | collective-permute-done | bytes 544 | tf_op jit(solution)/shard_map/while/body/eval_jaxpr/ppermute | solution.py:24
  105.9 6.2 %collective-permute-done.2 = bf16[16,16]{0,1:T(8,128)(2,1)S(1)} collective-permute-done((bf16[16,16]{0,1:T(8,128)(2,1)S(1)}, bf16[16,16]{0,1:T(8,128)(2,1)S(1)}, u32[]{:S(2)}, u32[]{:S(2)}) %collective-permute-start.2) | collective-permute-done | bytes 544 | tf_op jit(solution)/shard_map/while/body/eval_jaxpr/ppermute | solution.py:24
  113.6 6.2 %collective-permute-done.2 = bf16[16,16]{0,1:T(8,128)(2,1)S(1)} collective-permute-done((bf16[16,16]{0,1:T(8,128)(2,1)S(1)}, bf16[16,16]{0,1:T(8,128)(2,1)S(1)}, u32[]{:S(2)}, u32[]{:S(2)}) %collective-permute-start.2) | collective-permute-done | bytes 544 | tf_op jit(solution)/shard_map/while/body/eval_jaxpr/ppermute | solution.py:24
  121.4 6.2 %collective-permute-done.2 = bf16[16,16]{0,1:T(8,128)(2,1)S(1)} collective-permute-done((bf16[16,16]{0,1:T(8,128)(2,1)S(1)}, bf16[16,16]{0,1:T(8,128)(2,1)S(1)}, u32[]{:S(2)}, u32[]{:S(2)}) %collective-permute-start.2) | collective-permute-done | bytes 544 | tf_op jit(solution)/shard_map/while/body/eval_jaxpr/ppermute | solution.py:24
  129.1 6.2 %collective-permute-done.2 = bf16[16,16]{0,1:T(8,128)(2,1)S(1)} collective-permute-done((bf16[16,16]{0,1:T(8,128)(2,1)S(1)}, bf16[16,16]{0,1:T(8,128)(2,1)S(1)}, u32[]{:S(2)}, u32[]{:S(2)}) %collective-permute-start.2) | collective-permute-done | bytes 544 | tf_op jit(solution)/shard_map/while/body/eval_jaxpr/ppermute | solution.py:24
  136.9 6.2 %collective-permute-done.2 = bf16[16,16]{0,1:T(8,128)(2,1)S(1)} collective-permute-done((bf16[16,16]{0,1:T(8,128)(2,1)S(1)}, bf16[16,16]{0,1:T(8,128)(2,1)S(1)}, u32[]{:S(2)}, u32[]{:S(2)}) %collective-permute-start.2) | collective-permute-done | bytes 544 | tf_op jit(solution)/shard_map/while/body/eval_jaxpr/ppermute | solution.py:24
  144.7 6.2 %collective-permute-done.2 = bf16[16,16]{0,1:T(8,128)(2,1)S(1)} collective-permute-done((bf16[16,16]{0,1:T(8,128)(2,1)S(1)}, bf16[16,16]{0,1:T(8,128)(2,1)S(1)}, u32[]{:S(2)}, u32[]{:S(2)}) %collective-permute-start.2) | collective-permute-done | bytes 544 | tf_op jit(solution)/shard_map/while/body/eval_jaxpr/ppermute | solution.py:24
  152.4 6.2 %collective-permute-done.2 = bf16[16,16]{0,1:T(8,128)(2,1)S(1)} collective-permute-done((bf16[16,16]{0,1:T(8,128)(2,1)S(1)}, bf16[16,16]{0,1:T(8,128)(2,1)S(1)}, u32[]{:S(2)}, u32[]{:S(2)}) %collective-permute-start.2) | collective-permute-done | bytes 544 | tf_op jit(solution)/shard_map/while/body/eval_jaxpr/ppermute | solution.py:24
  160.2 6.2 %collective-permute-done.2 = bf16[16,16]{0,1:T(8,128)(2,1)S(1)} collective-permute-done((bf16[16,16]{0,1:T(8,128)(2,1)S(1)}, bf16[16,16]{0,1:T(8,128)(2,1)S(1)}, u32[]{:S(2)}, u32[]{:S(2)}) %collective-permute-start.2) | collective-permute-done | bytes 544 | tf_op jit(solution)/shard_map/while/body/eval_jaxpr/ppermute | solution.py:24
  168.0 6.2 %collective-permute-done.2 = bf16[16,16]{0,1:T(8,128)(2,1)S(1)} collective-permute-done((bf16[16,16]{0,1:T(8,128)(2,1)S(1)}, bf16[16,16]{0,1:T(8,128)(2,1)S(1)}, u32[]{:S(2)}, u32[]{:S(2)}) %collective-permute-start.2) | collective-permute-done | bytes 544 | tf_op jit(solution)/shard_map/while/body/eval_jaxpr/ppermute | solution.py:24
  175.7 6.2 %collective-permute-done.2 = bf16[16,16]{0,1:T(8,128)(2,1)S(1)} collective-permute-done((bf16[16,16]{0,1:T(8,128)(2,1)S(1)}, bf16[16,16]{0,1:T(8,128)(2,1)S(1)}, u32[]{:S(2)}, u32[]{:S(2)}) %collective-permute-start.2) | collective-permute-done | bytes 544 | tf_op jit(solution)/shard_map/while/body/eval_jaxpr/ppermute | solution.py:24
  183.3 6.0 %collective-permute-done.5 = bf16[16,16]{0,1:T(8,128)(2,1)S(1)} collective-permute-done((bf16[16,16]{0,1:T(8,128)(2,1)S(1)}, bf16[16,16]{0,1:T(8,128)(2,1)S(1)}, u32[]{:S(2)}, u32[]{:S(2)}) %collective-permute-start.5) | collective-permute-done | bytes 544 | tf_op jit(solution)/shard_map/ppermute | solution.py:24
  189.6 2.6 %fusion.13 = bf16[16,1024]{1,0:T(8,128)(2,1)} fusion(bf16[1024,1024]{1,0:T(8,128)(2,1)} %param.19, bf16[16,1024]{1,0:T(8,128)(2,1)S(1)} %copy-done.1, f32[16,1024]{1,0:T(8,128)S(1)} %div.36, bf16[16,1024]{1,0:T(8,128)(2,1)S(1)} %collective-permute-done.4), kind=kOutput, calls=%fused_computation.29 | convolution fusion | flops 33652736 | bytes 2260992 | tf_op jit(solution)/shard_map/dot_general | solution.py:116
  (383 shorter events, 53.2 us)
Async XLA Ops:
  1.6 23.8 %all-to-all-start.1 = ((s32[32,16,1]{0,2,1:T(1,128)}), s32[32,16,1]{0,2,1:T(1,128)S(1)}, u32[]{:S(2)}, u32[]{:S(2)}) async-start(s32[32,16,1]{0,2,1:T(1,128)} %copy.69), calls=%async_computation.1 | async-start | bytes 16384 | tf_op jit(solution)/shard_map/all_to_all | solution.py:71
  25.4 29.0 %all-to-all-start = ((bf16[16,32,1,1024]{3,1,2,0:T(8,128)(2,1)}), bf16[16,32,1,1024]{3,1,2,0:T(8,128)(2,1)}, u32[]{:S(2)}, u32[]{:S(2)}) async-start(bf16[16,32,1,1024]{3,1,2,0:T(8,128)(2,1)} %bitcast_dynamic-update-slice_fusion), calls=%async_computation | async-start | bytes 2097152 | tf_op jit(solution)/shard_map/all_to_all | solution.py:14
  64.8 8.5 %collective-permute-start.3 = (bf16[16,1024]{1,0:T(8,128)(2,1)S(1)}, bf16[16,1024]{1,0:T(8,128)(2,1)S(1)}, u32[]{:S(2)}, u32[]{:S(2)}) collective-permute-start(bf16[16,1024]{1,0:T(8,128)(2,1)S(1)} %convert_element_type.136), channel_id=1, source_target_pairs={{15,0},{0,1},{1,2},{2,3},{3,4},{4,5},{5,6},{6,7},{7,8},{8,9},{9,10... | collective-permute-start | bytes 98312 | tf_op jit(solution)/shard_map/while/body/eval_jaxpr/ppermute | solution.py:24
  65.5 7.8 %collective-permute-start = (bf16[16,1024]{1,0:T(8,128)(2,1)S(1)}, bf16[16,1024]{1,0:T(8,128)(2,1)S(1)}, u32[]{:S(2)}, u32[]{:S(2)}) collective-permute-start(bf16[16,1024]{1,0:T(8,128)(2,1)S(1)} %copy.150), channel_id=1, source_target_pairs={{15,0},{0,1},{1,2},{2,3},{3,4},{4,5},{5,6},{6,7},{7,8},{8,9},{9,10... | collective-permute-start | bytes 98312 | tf_op jit(solution)/shard_map/while/body/eval_jaxpr/ppermute | solution.py:24
  74.5 6.5 %collective-permute-start.3 = (bf16[16,1024]{1,0:T(8,128)(2,1)S(1)}, bf16[16,1024]{1,0:T(8,128)(2,1)S(1)}, u32[]{:S(2)}, u32[]{:S(2)}) collective-permute-start(bf16[16,1024]{1,0:T(8,128)(2,1)S(1)} %convert_element_type.136), channel_id=1, source_target_pairs={{15,0},{0,1},{1,2},{2,3},{3,4},{4,5},{5,6},{6,7},{7,8},{8,9},{9,10... | collective-permute-start | bytes 98312 | tf_op jit(solution)/shard_map/while/body/eval_jaxpr/ppermute | solution.py:24
  74.6 6.5 %collective-permute-start = (bf16[16,1024]{1,0:T(8,128)(2,1)S(1)}, bf16[16,1024]{1,0:T(8,128)(2,1)S(1)}, u32[]{:S(2)}, u32[]{:S(2)}) collective-permute-start(bf16[16,1024]{1,0:T(8,128)(2,1)S(1)} %copy.150), channel_id=1, source_target_pairs={{15,0},{0,1},{1,2},{2,3},{3,4},{4,5},{5,6},{6,7},{7,8},{8,9},{9,10... | collective-permute-start | bytes 98312 | tf_op jit(solution)/shard_map/while/body/eval_jaxpr/ppermute | solution.py:24
  82.3 6.5 %collective-permute-start.3 = (bf16[16,1024]{1,0:T(8,128)(2,1)S(1)}, bf16[16,1024]{1,0:T(8,128)(2,1)S(1)}, u32[]{:S(2)}, u32[]{:S(2)}) collective-permute-start(bf16[16,1024]{1,0:T(8,128)(2,1)S(1)} %convert_element_type.136), channel_id=1, source_target_pairs={{15,0},{0,1},{1,2},{2,3},{3,4},{4,5},{5,6},{6,7},{7,8},{8,9},{9,10... | collective-permute-start | bytes 98312 | tf_op jit(solution)/shard_map/while/body/eval_jaxpr/ppermute | solution.py:24
  90.1 6.5 %collective-permute-start.3 = (bf16[16,1024]{1,0:T(8,128)(2,1)S(1)}, bf16[16,1024]{1,0:T(8,128)(2,1)S(1)}, u32[]{:S(2)}, u32[]{:S(2)}) collective-permute-start(bf16[16,1024]{1,0:T(8,128)(2,1)S(1)} %convert_element_type.136), channel_id=1, source_target_pairs={{15,0},{0,1},{1,2},{2,3},{3,4},{4,5},{5,6},{6,7},{7,8},{8,9},{9,10... | collective-permute-start | bytes 98312 | tf_op jit(solution)/shard_map/while/body/eval_jaxpr/ppermute | solution.py:24
  90.1 6.5 %collective-permute-start = (bf16[16,1024]{1,0:T(8,128)(2,1)S(1)}, bf16[16,1024]{1,0:T(8,128)(2,1)S(1)}, u32[]{:S(2)}, u32[]{:S(2)}) collective-permute-start(bf16[16,1024]{1,0:T(8,128)(2,1)S(1)} %copy.150), channel_id=1, source_target_pairs={{15,0},{0,1},{1,2},{2,3},{3,4},{4,5},{5,6},{6,7},{7,8},{8,9},{9,10... | collective-permute-start | bytes 98312 | tf_op jit(solution)/shard_map/while/body/eval_jaxpr/ppermute | solution.py:24
  97.8 6.5 %collective-permute-start.3 = (bf16[16,1024]{1,0:T(8,128)(2,1)S(1)}, bf16[16,1024]{1,0:T(8,128)(2,1)S(1)}, u32[]{:S(2)}, u32[]{:S(2)}) collective-permute-start(bf16[16,1024]{1,0:T(8,128)(2,1)S(1)} %convert_element_type.136), channel_id=1, source_target_pairs={{15,0},{0,1},{1,2},{2,3},{3,4},{4,5},{5,6},{6,7},{7,8},{8,9},{9,10... | collective-permute-start | bytes 98312 | tf_op jit(solution)/shard_map/while/body/eval_jaxpr/ppermute | solution.py:24
  97.9 6.5 %collective-permute-start = (bf16[16,1024]{1,0:T(8,128)(2,1)S(1)}, bf16[16,1024]{1,0:T(8,128)(2,1)S(1)}, u32[]{:S(2)}, u32[]{:S(2)}) collective-permute-start(bf16[16,1024]{1,0:T(8,128)(2,1)S(1)} %copy.150), channel_id=1, source_target_pairs={{15,0},{0,1},{1,2},{2,3},{3,4},{4,5},{5,6},{6,7},{7,8},{8,9},{9,10... | collective-permute-start | bytes 98312 | tf_op jit(solution)/shard_map/while/body/eval_jaxpr/ppermute | solution.py:24
  105.6 6.5 %collective-permute-start.3 = (bf16[16,1024]{1,0:T(8,128)(2,1)S(1)}, bf16[16,1024]{1,0:T(8,128)(2,1)S(1)}, u32[]{:S(2)}, u32[]{:S(2)}) collective-permute-start(bf16[16,1024]{1,0:T(8,128)(2,1)S(1)} %convert_element_type.136), channel_id=1, source_target_pairs={{15,0},{0,1},{1,2},{2,3},{3,4},{4,5},{5,6},{6,7},{7,8},{8,9},{9,10... | collective-permute-start | bytes 98312 | tf_op jit(solution)/shard_map/while/body/eval_jaxpr/ppermute | solution.py:24
  105.7 6.5 %collective-permute-start = (bf16[16,1024]{1,0:T(8,128)(2,1)S(1)}, bf16[16,1024]{1,0:T(8,128)(2,1)S(1)}, u32[]{:S(2)}, u32[]{:S(2)}) collective-permute-start(bf16[16,1024]{1,0:T(8,128)(2,1)S(1)} %copy.150), channel_id=1, source_target_pairs={{15,0},{0,1},{1,2},{2,3},{3,4},{4,5},{5,6},{6,7},{7,8},{8,9},{9,10... | collective-permute-start | bytes 98312 | tf_op jit(solution)/shard_map/while/body/eval_jaxpr/ppermute | solution.py:24
  113.4 6.5 %collective-permute-start.3 = (bf16[16,1024]{1,0:T(8,128)(2,1)S(1)}, bf16[16,1024]{1,0:T(8,128)(2,1)S(1)}, u32[]{:S(2)}, u32[]{:S(2)}) collective-permute-start(bf16[16,1024]{1,0:T(8,128)(2,1)S(1)} %convert_element_type.136), channel_id=1, source_target_pairs={{15,0},{0,1},{1,2},{2,3},{3,4},{4,5},{5,6},{6,7},{7,8},{8,9},{9,10... | collective-permute-start | bytes 98312 | tf_op jit(solution)/shard_map/while/body/eval_jaxpr/ppermute | solution.py:24
  121.1 6.5 %collective-permute-start.3 = (bf16[16,1024]{1,0:T(8,128)(2,1)S(1)}, bf16[16,1024]{1,0:T(8,128)(2,1)S(1)}, u32[]{:S(2)}, u32[]{:S(2)}) collective-permute-start(bf16[16,1024]{1,0:T(8,128)(2,1)S(1)} %convert_element_type.136), channel_id=1, source_target_pairs={{15,0},{0,1},{1,2},{2,3},{3,4},{4,5},{5,6},{6,7},{7,8},{8,9},{9,10... | collective-permute-start | bytes 98312 | tf_op jit(solution)/shard_map/while/body/eval_jaxpr/ppermute | solution.py:24
  121.2 6.5 %collective-permute-start = (bf16[16,1024]{1,0:T(8,128)(2,1)S(1)}, bf16[16,1024]{1,0:T(8,128)(2,1)S(1)}, u32[]{:S(2)}, u32[]{:S(2)}) collective-permute-start(bf16[16,1024]{1,0:T(8,128)(2,1)S(1)} %copy.150), channel_id=1, source_target_pairs={{15,0},{0,1},{1,2},{2,3},{3,4},{4,5},{5,6},{6,7},{7,8},{8,9},{9,10... | collective-permute-start | bytes 98312 | tf_op jit(solution)/shard_map/while/body/eval_jaxpr/ppermute | solution.py:24
  128.9 6.5 %collective-permute-start.3 = (bf16[16,1024]{1,0:T(8,128)(2,1)S(1)}, bf16[16,1024]{1,0:T(8,128)(2,1)S(1)}, u32[]{:S(2)}, u32[]{:S(2)}) collective-permute-start(bf16[16,1024]{1,0:T(8,128)(2,1)S(1)} %convert_element_type.136), channel_id=1, source_target_pairs={{15,0},{0,1},{1,2},{2,3},{3,4},{4,5},{5,6},{6,7},{7,8},{8,9},{9,10... | collective-permute-start | bytes 98312 | tf_op jit(solution)/shard_map/while/body/eval_jaxpr/ppermute | solution.py:24
  128.9 6.5 %collective-permute-start = (bf16[16,1024]{1,0:T(8,128)(2,1)S(1)}, bf16[16,1024]{1,0:T(8,128)(2,1)S(1)}, u32[]{:S(2)}, u32[]{:S(2)}) collective-permute-start(bf16[16,1024]{1,0:T(8,128)(2,1)S(1)} %copy.150), channel_id=1, source_target_pairs={{15,0},{0,1},{1,2},{2,3},{3,4},{4,5},{5,6},{6,7},{7,8},{8,9},{9,10... | collective-permute-start | bytes 98312 | tf_op jit(solution)/shard_map/while/body/eval_jaxpr/ppermute | solution.py:24
  136.6 6.5 %collective-permute-start.3 = (bf16[16,1024]{1,0:T(8,128)(2,1)S(1)}, bf16[16,1024]{1,0:T(8,128)(2,1)S(1)}, u32[]{:S(2)}, u32[]{:S(2)}) collective-permute-start(bf16[16,1024]{1,0:T(8,128)(2,1)S(1)} %convert_element_type.136), channel_id=1, source_target_pairs={{15,0},{0,1},{1,2},{2,3},{3,4},{4,5},{5,6},{6,7},{7,8},{8,9},{9,10... | collective-permute-start | bytes 98312 | tf_op jit(solution)/shard_map/while/body/eval_jaxpr/ppermute | solution.py:24
  144.4 6.5 %collective-permute-start.3 = (bf16[16,1024]{1,0:T(8,128)(2,1)S(1)}, bf16[16,1024]{1,0:T(8,128)(2,1)S(1)}, u32[]{:S(2)}, u32[]{:S(2)}) collective-permute-start(bf16[16,1024]{1,0:T(8,128)(2,1)S(1)} %convert_element_type.136), channel_id=1, source_target_pairs={{15,0},{0,1},{1,2},{2,3},{3,4},{4,5},{5,6},{6,7},{7,8},{8,9},{9,10... | collective-permute-start | bytes 98312 | tf_op jit(solution)/shard_map/while/body/eval_jaxpr/ppermute | solution.py:24
  152.2 6.5 %collective-permute-start.3 = (bf16[16,1024]{1,0:T(8,128)(2,1)S(1)}, bf16[16,1024]{1,0:T(8,128)(2,1)S(1)}, u32[]{:S(2)}, u32[]{:S(2)}) collective-permute-start(bf16[16,1024]{1,0:T(8,128)(2,1)S(1)} %convert_element_type.136), channel_id=1, source_target_pairs={{15,0},{0,1},{1,2},{2,3},{3,4},{4,5},{5,6},{6,7},{7,8},{8,9},{9,10... | collective-permute-start | bytes 98312 | tf_op jit(solution)/shard_map/while/body/eval_jaxpr/ppermute | solution.py:24
  159.9 6.5 %collective-permute-start.3 = (bf16[16,1024]{1,0:T(8,128)(2,1)S(1)}, bf16[16,1024]{1,0:T(8,128)(2,1)S(1)}, u32[]{:S(2)}, u32[]{:S(2)}) collective-permute-start(bf16[16,1024]{1,0:T(8,128)(2,1)S(1)} %convert_element_type.136), channel_id=1, source_target_pairs={{15,0},{0,1},{1,2},{2,3},{3,4},{4,5},{5,6},{6,7},{7,8},{8,9},{9,10... | collective-permute-start | bytes 98312 | tf_op jit(solution)/shard_map/while/body/eval_jaxpr/ppermute | solution.py:24
  167.7 6.5 %collective-permute-start.3 = (bf16[16,1024]{1,0:T(8,128)(2,1)S(1)}, bf16[16,1024]{1,0:T(8,128)(2,1)S(1)}, u32[]{:S(2)}, u32[]{:S(2)}) collective-permute-start(bf16[16,1024]{1,0:T(8,128)(2,1)S(1)} %convert_element_type.136), channel_id=1, source_target_pairs={{15,0},{0,1},{1,2},{2,3},{3,4},{4,5},{5,6},{6,7},{7,8},{8,9},{9,10... | collective-permute-start | bytes 98312 | tf_op jit(solution)/shard_map/while/body/eval_jaxpr/ppermute | solution.py:24
  175.5 6.5 %collective-permute-start.3 = (bf16[16,1024]{1,0:T(8,128)(2,1)S(1)}, bf16[16,1024]{1,0:T(8,128)(2,1)S(1)}, u32[]{:S(2)}, u32[]{:S(2)}) collective-permute-start(bf16[16,1024]{1,0:T(8,128)(2,1)S(1)} %convert_element_type.136), channel_id=1, source_target_pairs={{15,0},{0,1},{1,2},{2,3},{3,4},{4,5},{5,6},{6,7},{7,8},{8,9},{9,10... | collective-permute-start | bytes 98312 | tf_op jit(solution)/shard_map/while/body/eval_jaxpr/ppermute | solution.py:24
  (45 other events, 354.2 us)
